TPU v7x, 256 devices: a whole 4x4x8 slice. The times are simulated.
256 devices in a mesh: ctx: 32 (over x, z), head: 8 (over y, core).
Axes of the slice: x: 4, y: 4, z: 8, core: 2. Of those that a mesh axis runs over, the one named last changes fastest.
Arguments:
- features: bfloat16 [8192, 16384], P('ctx', 'head'), may hold values from -6 to 6
- log_decay: float32 [256, 8192], P('head', 'ctx'), may hold values from -2 to 0, as said below
- step_size: float32 [256, 8192], P('head', 'ctx'), may hold values from 0.0002 to 0.002
- b_matrix: bfloat16 [8192, 2048], P('ctx', 'head'), may hold values from -6 to 6
- c_matrix: bfloat16 [8192, 2048], P('ctx', 'head'), may hold values from -6 to 6
- skip_gain: float32 [256], P('head'), may hold values from 0.5 to 1.5
Outputs:
- mixed: bfloat16 [8192, 16384], P('ctx', 'head')
Inputs may be any that keep to these rules, and one draw needn't show every extreme that they name: `log_decay`: every entry is negative.
All inputs are finite; a program needn't handle non-finite values.
Results may differ from a plain program's by a relative error of at most 0.0013.
Values sent between devices are 32-bit elements; how exact they have to be, the bound alone decides.
No kernel may reach another device: no remote copies, remote signals or barrier semaphores. Data moves between devices by JAX's collectives and lax.ppermute only.
A program may use at most 320 MiB of HBM per device.

v0:
```python
import jax
import jax.numpy as jnp
import numpy as np
from jax import lax
from jax.sharding import PartitionSpec as P

N = 256
SPAN = 128


def chain_mixing(decay, devices, halves):
    j = np.arange(devices)
    pos = np.stack([j, halves * devices - 1 - j], axis=1).reshape(-1)
    between = (pos[None, :, None] < pos[None, None, :]) & (pos[None, None, :] < pos[:, None, None])
    gap = jnp.sum(jnp.where(between[None], decay[:, None, None, :], 0.0), axis=-1)
    lower = pos[None, :] < pos[:, None]
    mixing = jnp.where(lower[None], jnp.exp(gap), 0.0)
    return mixing.reshape(-1, devices, halves, devices, halves)


def on_device(features, log_decay, step_size, b_matrix, c_matrix, skip_gain):
    head_count = log_decay.shape[0]
    tok_rows = features.shape[0]
    head_width = features.shape[1] // head_count
    state_size = N
    group_count = b_matrix.shape[1] // state_size
    per_group = head_count // group_count
    halves = tok_rows // SPAN
    assert halves == 2
    devices = lax.axis_size("ctx")
    per_chunk = head_count // devices
    flat = head_width * state_size
    rows = halves * head_width
    extra = 8
    cumulative = jnp.cumsum(log_decay.reshape(head_count, halves, SPAN), axis=2)
    totals = cumulative[:, :, -1]
    step_rows = step_size.reshape(head_count, halves, SPAN)
    grouped_inputs = features.reshape(halves, SPAN, group_count, per_group, head_width)
    b_spans = b_matrix.reshape(halves, SPAN, group_count, state_size)
    c_spans = c_matrix.reshape(halves, SPAN, group_count, state_size)
    coeffs = jnp.exp(totals[:, :, None] - cumulative) * step_rows
    coeffs = jnp.transpose(coeffs.reshape(group_count, per_group, halves, SPAN), (2, 3, 0, 1))
    weighted = (grouped_inputs * coeffs[..., None]).astype(jnp.bfloat16)
    span_states = jnp.einsum(
        "ksgn,ksgqp->gqkpn", b_spans, weighted, preferred_element_type=jnp.float32
    ).reshape(head_count, rows, state_size)
    me = lax.axis_index("ctx")
    spread = jnp.zeros((devices, halves, head_count), jnp.float32)
    spread = lax.dynamic_update_slice_in_dim(spread, jnp.transpose(totals)[None], me, axis=0)
    all_decay = lax.psum(spread, "ctx")
    got = lax.all_to_all(span_states, "ctx", 0, 0, tiled=True)
    got_states = got.reshape(devices, per_chunk, halves, head_width, state_size)
    mine = lax.dynamic_slice_in_dim(all_decay, me * per_chunk, per_chunk, axis=2)
    mixing = chain_mixing(
        jnp.transpose(mine, (2, 0, 1)).reshape(per_chunk, devices * halves), devices, halves
    )
    j = np.arange(devices)
    own = np.zeros((devices, halves, devices, halves), bool)
    own[j, 1, j, 0] = True
    others = jnp.where(own[None], 0.0, mixing)
    if per_chunk == 1:
        solved = jnp.einsum(
            "uv,vpn->upn",
            others.reshape(devices * halves, devices * halves),
            got.reshape(devices * halves, head_width, state_size),
            precision=lax.Precision.HIGHEST,
            preferred_element_type=jnp.float32,
        ).reshape(devices, rows, state_size)
    else:
        solved = jnp.einsum(
            "cjkJL,JcLpn->jckpn",
            others,
            got_states,
            precision=lax.Precision.HIGHEST,
            preferred_element_type=jnp.float32,
        ).reshape(devices * per_chunk, rows, state_size)
    back = lax.all_to_all(solved, "ctx", 0, 0, tiled=True)
    later = np.arange(devices)[:, None] > me
    gain = jnp.exp(jnp.sum(jnp.where(later, jnp.sum(all_decay, axis=1), 0.0), axis=0))
    state_halves = [
        back[:, :head_width].astype(jnp.bfloat16).reshape(head_count * head_width, state_size),
        (back[:, head_width:rows] + gain[:, None, None] * span_states[:, :head_width])
        .astype(jnp.bfloat16)
        .reshape(head_count * head_width, state_size),
    ]
    scores = jnp.einsum("ktgn,ksgn->gkts", c_spans, b_spans, preferred_element_type=jnp.float32)
    causal = jnp.arange(SPAN)[:, None] >= jnp.arange(SPAN)[None, :]
    cum_grouped = cumulative.reshape(group_count, per_group, halves, SPAN)
    step_grouped = step_rows.reshape(group_count, per_group, halves, SPAN)
    decay_gaps = jnp.where(causal, cum_grouped[..., :, None] - cum_grouped[..., None, :], -jnp.inf)
    weights = (scores[:, None] * jnp.exp(decay_gaps) * step_grouped[:, :, :, None, :]).astype(
        jnp.bfloat16
    )
    diagonal_part = jnp.einsum(
        "gqkts,ksgqp->ktgqp", weights, grouped_inputs, preferred_element_type=jnp.float32
    ).reshape(halves, SPAN, head_count * head_width)
    decay_in = jnp.repeat(jnp.transpose(jnp.exp(cumulative), (1, 2, 0)), head_width, axis=2)
    skip = jnp.repeat(skip_gain, head_width)[None, :]
    inputs = features.reshape(halves, SPAN, head_count * head_width).astype(jnp.float32)
    per_group_width = per_group * head_width
    outs = []
    for k in range(halves):
        state_part = jnp.concatenate(
            [
                jnp.dot(
                    c_spans[k, :, g],
                    state_halves[k][g * per_group_width : (g + 1) * per_group_width].T,
                    preferred_element_type=jnp.float32,
                )
                for g in range(group_count)
            ],
            axis=1,
        )
        outs.append(diagonal_part[k] + state_part * decay_in[k] + skip * inputs[k])
    return jnp.concatenate(outs, axis=0).astype(jnp.bfloat16)


def solution(mesh):
    placed = (
        P("ctx", "head"),
        P("head", "ctx"),
        P("head", "ctx"),
        P("ctx", "head"),
        P("ctx", "head"),
        P("head"),
    )
    return jax.shard_map(
        on_device, mesh=mesh, in_specs=placed, out_specs=P("ctx", "head"), check_vma=False
    )
```

profile of v0, /device:TPU:16, one launch (start us, length us, event | category | flops | bytes accessed | tf_op | source)
XLA Modules:
  0.0 344.3 jit_solution(12947823522675433255)
XLA Ops:
  0.0 0.8 copy_bitcast_fusion.1
  0.8 0.6 reduce_window_sum.13
  1.5 0.8 reshape.145
  2.4 1.5 copy.52
  4.2 1.1 multiply_convert_fusion.2
  5.3 0.7 convolution_bitcast_fusion.2
  6.0 2.2 copy.58
  8.3 11.6 %all-to-all-start = ((f32[32,128,256]{2,1,0:T(8,128)}), f32[32,128,256]{2,1,0:T(8,128)}, u32[]{:S(2)}, u32[]{:S(2)}) async-start(f32[32,128,256]{2,1,0:T(8,128)} %bitcast.92), calls=%async_computation | async-start | bytes 8388608 | tf_op jit(solution)/shard_map/all_to_all | solution.py:51
  20.1 232.9 %psum.7 = f32[32,2,32]{1,0,2:T(8,128)S(1)} all-reduce(f32[32,2,32]{1,0,2:T(8,128)S(1)} %dynamic_update_slice.3), channel_id=1, replica_groups=mesh['ctx'=32,'head'=8] {'ctx'}, use_global_device_ids=true, to_apply=%region_1.2 | all-reduce | flops 2048 | bytes 16384 | tf_op jit(solution)/shard_map/psum | solution.py:50
  253.1 0.6 select_reduce_fusion
  253.8 8.4 %fusion = f32[64,64,256]{2,0,1:T(8,128)S(1)} fusion(f32[64,64,256]{2,1,0:T(8,128)} %bitcast.17, pred[64,64]{1,0:T(32,128)(4,1)S(1)} %copy-done.11, pred[64,64]{1,0:T(32,128)(4,1)S(1)} %copy-done.10, f32[64,64]{1,0:T(8,128)S(1)} %select_reduce_fusion), kind=kOutput, calls=%fused_computation | convolution fusion | flops 805314560 | bytes 8413184 | tf_op jit(solution)/shard_map/uv,vpn->upn/dot_general | solution.py:62
  262.2 4.4 %copy.60 = f32[64,64,256]{2,1,0:T(8,128)} copy(f32[64,64,256]{2,0,1:T(8,128)S(1)} %fusion) | data formatting | bytes 8388608 | tf_op jit(solution)/shard_map/uv,vpn->upn/dot_general | solution.py:62
  266.6 5.2 %all-to-all-start.1 = ((f32[32,128,256]{2,1,0:T(8,128)}), f32[32,128,256]{2,1,0:T(8,128)}, u32[]{:S(2)}, u32[]{:S(2)}) async-start(f32[32,128,256]{2,1,0:T(8,128)} %bitcast.94), calls=%async_computation.1 | async-start | bytes 8388608 | tf_op jit(solution)/shard_map/all_to_all | solution.py:77
  272.6 3.6 %fusion.19 = f32[2,128,1,32,64]{1,4,3,0,2:T(8,128)S(1)} fusion(f32[32,2,128]{2,0,1:T(8,128)S(1)} %copy_bitcast_fusion, f32[32,2,128]{2,0,1:T(8,128)S(1)} %reduce_window_sum.13, f32[2,128,128]{2,1,0:T(8,128)S(1)} %fusion.35, pred[128,128]{1,0:T(8,128)(4,1)S(1)} %iota_compare_fusion, bf16[2,128,32,64]{1,0,3,2:T(2,128)(2,1)} %copy-done.2), kind=kOutput, calls=%fused_computation.27 | convolution fusion | flops 139460608 | bytes 3358720 | tf_op jit(solution)/shard_map/gqkts,ksgqp->ktgqp/dot_general | solution.py:94
  276.2 1.2 fusion.34
  277.4 1.3 copy.64
  278.8 1.3 copy.63
  280.3 2.6 copy.62
  283.0 1.3 copy.61
  284.3 53.5 %all-to-all-done.1 = f32[32,128,256]{2,1,0:T(8,128)} async-done(((f32[32,128,256]{2,1,0:T(8,128)}), f32[32,128,256]{2,1,0:T(8,128)}, u32[]{:S(2)}, u32[]{:S(2)}) %all-to-all-start.1) | async-done | bytes 4194336 | tf_op jit(solution)/shard_map/all_to_all | solution.py:77
  337.8 2.6 fusion.12
  340.4 0.5 fusion.8
  340.9 1.8 slice.95
  343.3 1.1 pad_maximum_fusion
  (53 shorter events, 2.5 us)
Async XLA Ops:
  0.0 5.3 %copy-start = (bf16[256,256]{1,0:T(8,128)(2,1)S(1)}, bf16[256,256]{1,0:T(8,128)(2,1)}, u32[]{:S(2)}) copy-start(bf16[256,256]{1,0:T(8,128)(2,1)} %param.13) | copy-start | bytes 393220
  4.2 4.0 %copy-start.2 = (bf16[2,128,32,64]{1,0,3,2:T(2,128)(2,1)}, bf16[2,128,32,64]{1,0,3,2:T(2,128)(2,1)S(1)}, u32[]{:S(2)}) copy-start(bf16[2,128,32,64]{1,0,3,2:T(2,128)(2,1)S(1)} %reshape.142) | copy-start | bytes 3145732
  8.3 244.9 %copy-start.8 = (pred[1,64,64,64]{3,2,1,0:T(32,128)(4,1)S(1)}, pred[1,64,64,64]{3,2,1,0:T(32,128)(4,1)}, u32[]{:S(2)}) copy-start(pred[1,64,64,64]{3,2,1,0:T(32,128)(4,1)} %constant.26.clone) | copy-start | bytes 786436
  8.3 245.5 %copy-start.10 = (pred[64,64]{1,0:T(32,128)(4,1)S(1)}, pred[64,64]{1,0:T(32,128)(4,1)}, u32[]{:S(2)}) copy-start(pred[64,64]{1,0:T(32,128)(4,1)} %constant.31) | copy-start | bytes 12292
  8.3 245.5 %copy-start.11 = (pred[64,64]{1,0:T(32,128)(4,1)S(1)}, pred[64,64]{1,0:T(32,128)(4,1)}, u32[]{:S(2)}) copy-start(pred[64,64]{1,0:T(32,128)(4,1)} %constant.32) | copy-start | bytes 12292
  8.3 245.5 %all-to-all-start = ((f32[32,128,256]{2,1,0:T(8,128)}), f32[32,128,256]{2,1,0:T(8,128)}, u32[]{:S(2)}, u32[]{:S(2)}) async-start(f32[32,128,256]{2,1,0:T(8,128)} %bitcast.92), calls=%async_computation | async-start | bytes 8388608 | tf_op jit(solution)/shard_map/all_to_all | solution.py:51
  266.6 5.4 %copy-start.1 = (bf16[256,2048]{1,0:T(8,128)(2,1)S(1)}, bf16[256,2048]{1,0:T(8,128)(2,1)}, u32[]{:S(2)}) copy-start(bf16[256,2048]{1,0:T(8,128)(2,1)} %param.10) | copy-start | bytes 3145732
  266.6 5.7 %copy-start.13 = (s32[32,1]{0,1:T(1,128)S(1)}, s32[32,1]{0,1:T(1,128)}, u32[]{:S(2)}) copy-start(s32[32,1]{0,1:T(1,128)} %constant.29.clone) | copy-start | bytes 388
  266.6 5.8 %copy-start.9 = (f32[32,256]{1,0:T(8,128)S(1)}, f32[32,256]{1,0:T(8,128)}, u32[]{:S(2)}) copy-start(f32[32,256]{1,0:T(8,128)} %param.12) | copy-start | bytes 98308
  266.6 5.9 %copy-start.7 = (bf16[256,256]{1,0:T(8,128)(2,1)S(1)}, bf16[256,256]{1,0:T(8,128)(2,1)}, u32[]{:S(2)}) copy-start(bf16[256,256]{1,0:T(8,128)(2,1)} %param.14) | copy-start | bytes 393220
  266.6 71.2 %all-to-all-start.1 = ((f32[32,128,256]{2,1,0:T(8,128)}), f32[32,128,256]{2,1,0:T(8,128)}, u32[]{:S(2)}, u32[]{:S(2)}) async-start(f32[32,128,256]{2,1,0:T(8,128)} %bitcast.94), calls=%async_computation.1 | async-start | bytes 8388608 | tf_op jit(solution)/shard_map/all_to_all | solution.py:77
  276.2 3.9 %copy-start.12 = (f32[32]{0:T(128)S(1)}, f32[32]{0:T(128)}, u32[]{:S(2)}) copy-start(f32[32]{0:T(128)} %param.15) | copy-start | bytes 388
  284.3 56.1 %copy-start.3 = (f32[128,2048]{1,0:T(8,128)S(1)}, f32[128,2048]{1,0:T(8,128)}, u32[]{:S(2)}) copy-start(f32[128,2048]{1,0:T(8,128)} %copy.64) | copy-start | bytes 3145732
  337.8 2.6 copy-start.5
  340.4 2.4 copy-start.4
  340.4 2.4 copy-start.6
where the time goes:
time: 345 us; the launch traced here: 344 us
  blocking collectives  233 us (68%)
  waiting for transfers between devices  53.5 us (16%)
  local copies, waits for them, and re-layouts  20.4 us (6%)
  starting transfers between devices  16.8 us (5%)
  matrix products  13.9 us (4%)
  other arithmetic  6.54 us (2%)
    psum x1, blocking collectives, on_device(): all_decay = lax.psum(spread, 'ctx')  233 us
    all_to_all x1, waiting for transfers between devices, on_device(): back = lax.all_to_all(solved, 'ctx', 0, 0, tiled=True)  53.5 us
    all_to_all x1, starting transfers between devices, on_device(): got = lax.all_to_all(span_states, 'ctx', 0, 0, tiled=True)  11.6 us
    dot_general x1, matrix products, on_device(): jnp.einsum('uv,vpn->upn', others.reshape(devices * halves, devices * halv...  8.4 us
  transfers between devices with their start and end apart: 2, of which 1 were waited for; matrix products, arithmetic and copies ran while one was open for 4% of the time, Pallas kernels for 0%

commit v1 on v0

--- a/solution.py
+++ b/solution.py
@@ -6,6 +6,10 @@
 
 N = 256
 SPAN = 128
+
+
+def advance_unit(page, axis_tag):
+    return jnp.sum(lax.all_gather(page, axis_name=axis_tag), axis=0)
 
 
 def chain_mixing(decay, devices, halves):
@@ -47,7 +51,7 @@
     me = lax.axis_index("ctx")
     spread = jnp.zeros((devices, halves, head_count), jnp.float32)
     spread = lax.dynamic_update_slice_in_dim(spread, jnp.transpose(totals)[None], me, axis=0)
-    all_decay = lax.psum(spread, "ctx")
+    all_decay = advance_unit(spread, "ctx")
     got = lax.all_to_all(span_states, "ctx", 0, 0, tiled=True)
     got_states = got.reshape(devices, per_chunk, halves, head_width, state_size)
     mine = lax.dynamic_slice_in_dim(all_decay, me * per_chunk, per_chunk, axis=2)

time: 345 us -> 271 us (0.79)
  blocking collectives: 233 us -> 137 us
  waiting for transfers between devices: 53.5 us -> 73.6 us
    psum x1 -> x0, blocking collectives: 233 us -> none  [on_device(): all_decay = lax.psum(spread, 'ctx')]
    all_gather x0 -> x1, blocking collectives: none -> 137 us  [advance_unit(): return jnp.sum(lax.all_gather(page, axis_name=axis_tag), axis=0)]
    all_to_all x1, waiting for transfers between devices: 53.5 us -> 73.6 us  [on_device(): back = lax.all_to_all(solved, 'ctx', 0, 0, tiled=True)]
  transfers between devices with their start and end apart: 2 -> 2, of which waited for: 1 -> 1; matrix products, arithmetic and copies ran while one was open for 4% -> 5% of each run, Pallas kernels for 0% -> 0%
where the time goes in v1:
time: 271 us
  blocking collectives  137 us (51%)
  waiting for transfers between devices  73.6 us (27%)
  local copies, waits for them, and re-layouts  20.4 us (8%)
  starting transfers between devices  19.3 us (7%)
  matrix products  13.9 us (5%)
  other arithmetic  6.44 us (2%)
    all_gather x1, blocking collectives, advance_unit(): return jnp.sum(lax.all_gather(page, axis_name=axis_tag), axis=0)  137 us
    all_to_all x1, waiting for transfers between devices, on_device(): back = lax.all_to_all(solved, 'ctx', 0, 0, tiled=True)  73.6 us
    all_to_all x1, starting transfers between devices, on_device(): got = lax.all_to_all(span_states, 'ctx', 0, 0, tiled=True)  11.6 us
    dot_general x1, matrix products, on_device(): jnp.einsum('uv,vpn->upn', others.reshape(devices * halves, devices * halv...  8.4 us
    all_to_all x1, starting transfers between devices, on_device(): back = lax.all_to_all(solved, 'ctx', 0, 0, tiled=True)  7.7 us
  transfers between devices with their start and end apart: 2, of which 1 were waited for; matrix products, arithmetic and copies ran while one was open for 5% of the time, Pallas kernels for 0%

profile of v1, /device:TPU:16, one launch (start us, length us, event | category | flops | bytes accessed | tf_op | source)
XLA Modules:
  0.0 270.6 jit_solution(3616762329713386177)
XLA Ops:
  0.0 0.8 copy_bitcast_fusion.1
  0.8 0.6 reduce_window_sum.13
  1.5 0.8 reshape.148
  2.4 1.5 copy.51
  4.2 1.1 multiply_convert_fusion.2
  5.3 0.7 convolution_bitcast_fusion.2
  6.0 2.2 copy.58
  8.3 11.6 %all-to-all-start = ((f32[32,128,256]{2,1,0:T(8,128)}), f32[32,128,256]{2,1,0:T(8,128)}, u32[]{:S(2)}, u32[]{:S(2)}) async-start(f32[32,128,256]{2,1,0:T(8,128)} %bitcast.92), calls=%async_computation | async-start | bytes 8388608 | tf_op jit(solution)/shard_map/all_to_all | solution.py:55
  19.9 136.5 %all_gather.7 = f32[32,32,2,32]{3,1,2,0:T(8,128)S(1)} all-gather(f32[1,32,2,32]{3,1,2,0:T(8,128)S(1)} %dynamic_update_slice.4), channel_id=1, replica_groups=mesh['ctx'=32,'head'=8] {'ctx'}, dimensions={0}, use_global_device_ids=true | all-gather | bytes 270336 | tf_op jit(solution)/shard_map/all_gather | solution.py:12
  157.0 0.6 select_reduce_fusion
  157.6 8.4 %fusion = f32[64,64,256]{2,0,1:T(8,128)S(1)} fusion(f32[64,64,256]{2,1,0:T(8,128)} %bitcast.18, pred[64,64]{1,0:T(32,128)(4,1)S(1)} %copy-done.11, pred[64,64]{1,0:T(32,128)(4,1)S(1)} %copy-done.10, f32[64,64]{1,0:T(8,128)S(1)} %select_reduce_fusion), kind=kOutput, calls=%fused_computation | convolution fusion | flops 805314560 | bytes 8413184 | tf_op jit(solution)/shard_map/uv,vpn->upn/dot_general | solution.py:66
  166.0 4.4 %copy.60 = f32[64,64,256]{2,1,0:T(8,128)} copy(f32[64,64,256]{2,0,1:T(8,128)S(1)} %fusion) | data formatting | bytes 8388608 | tf_op jit(solution)/shard_map/uv,vpn->upn/dot_general | solution.py:66
  170.4 7.7 %all-to-all-start.1 = ((f32[32,128,256]{2,1,0:T(8,128)}), f32[32,128,256]{2,1,0:T(8,128)}, u32[]{:S(2)}, u32[]{:S(2)}) async-start(f32[32,128,256]{2,1,0:T(8,128)} %bitcast.94), calls=%async_computation.1 | async-start | bytes 8388608 | tf_op jit(solution)/shard_map/all_to_all | solution.py:81
  178.8 3.6 %fusion.19 = f32[2,128,1,32,64]{1,4,3,0,2:T(8,128)S(1)} fusion(f32[32,2,128]{2,0,1:T(8,128)S(1)} %copy_bitcast_fusion, f32[32,2,128]{2,0,1:T(8,128)S(1)} %reduce_window_sum.13, f32[2,128,128]{2,1,0:T(8,128)S(1)} %fusion.36, pred[128,128]{1,0:T(8,128)(4,1)S(1)} %iota_compare_fusion, bf16[2,128,32,64]{1,0,3,2:T(2,128)(2,1)} %copy-done.2), kind=kOutput, calls=%fused_computation.27 | convolution fusion | flops 139460608 | bytes 3358720 | tf_op jit(solution)/shard_map/gqkts,ksgqp->ktgqp/dot_general | solution.py:98
  182.4 1.2 fusion.35
  183.5 1.3 copy.64
  184.9 1.3 copy.63
  186.4 2.6 copy.62
  189.1 1.3 copy.61
  190.4 73.6 %all-to-all-done.1 = f32[32,128,256]{2,1,0:T(8,128)} async-done(((f32[32,128,256]{2,1,0:T(8,128)}), f32[32,128,256]{2,1,0:T(8,128)}, u32[]{:S(2)}, u32[]{:S(2)}) %all-to-all-start.1) | async-done | bytes 4194336 | tf_op jit(solution)/shard_map/all_to_all | solution.py:81
  264.0 2.6 fusion.12
  266.6 0.5 fusion.8
  267.2 1.8 slice.95
  269.5 1.1 pad_maximum_fusion
  (53 shorter events, 2.5 us)
Async XLA Ops:
  0.0 5.3 %copy-start = (bf16[256,256]{1,0:T(8,128)(2,1)S(1)}, bf16[256,256]{1,0:T(8,128)(2,1)}, u32[]{:S(2)}) copy-start(bf16[256,256]{1,0:T(8,128)(2,1)} %param.13) | copy-start | bytes 393220
  4.2 4.0 %copy-start.2 = (bf16[2,128,32,64]{1,0,3,2:T(2,128)(2,1)}, bf16[2,128,32,64]{1,0,3,2:T(2,128)(2,1)S(1)}, u32[]{:S(2)}) copy-start(bf16[2,128,32,64]{1,0,3,2:T(2,128)(2,1)S(1)} %reshape.145) | copy-start | bytes 3145732
  8.3 148.7 %copy-start.8 = (pred[1,64,64,64]{3,2,1,0:T(32,128)(4,1)S(1)}, pred[1,64,64,64]{3,2,1,0:T(32,128)(4,1)}, u32[]{:S(2)}) copy-start(pred[1,64,64,64]{3,2,1,0:T(32,128)(4,1)} %constant.27.clone) | copy-start | bytes 786436
  8.3 149.3 %copy-start.10 = (pred[64,64]{1,0:T(32,128)(4,1)S(1)}, pred[64,64]{1,0:T(32,128)(4,1)}, u32[]{:S(2)}) copy-start(pred[64,64]{1,0:T(32,128)(4,1)} %constant.32) | copy-start | bytes 12292
  8.3 149.3 %copy-start.11 = (pred[64,64]{1,0:T(32,128)(4,1)S(1)}, pred[64,64]{1,0:T(32,128)(4,1)}, u32[]{:S(2)}) copy-start(pred[64,64]{1,0:T(32,128)(4,1)} %constant.33) | copy-start | bytes 12292
  8.3 149.3 %all-to-all-start = ((f32[32,128,256]{2,1,0:T(8,128)}), f32[32,128,256]{2,1,0:T(8,128)}, u32[]{:S(2)}, u32[]{:S(2)}) async-start(f32[32,128,256]{2,1,0:T(8,128)} %bitcast.92), calls=%async_computation | async-start | bytes 8388608 | tf_op jit(solution)/shard_map/all_to_all | solution.py:55
  170.4 7.7 %copy-start.1 = (bf16[256,2048]{1,0:T(8,128)(2,1)S(1)}, bf16[256,2048]{1,0:T(8,128)(2,1)}, u32[]{:S(2)}) copy-start(bf16[256,2048]{1,0:T(8,128)(2,1)} %param.10) | copy-start | bytes 3145732
  170.4 8.0 %copy-start.13 = (s32[32,1]{0,1:T(1,128)S(1)}, s32[32,1]{0,1:T(1,128)}, u32[]{:S(2)}) copy-start(s32[32,1]{0,1:T(1,128)} %constant.30.clone) | copy-start | bytes 388
  170.4 8.1 %copy-start.9 = (f32[32,256]{1,0:T(8,128)S(1)}, f32[32,256]{1,0:T(8,128)}, u32[]{:S(2)}) copy-start(f32[32,256]{1,0:T(8,128)} %param.12) | copy-start | bytes 98308
  170.4 8.1 %copy-start.7 = (bf16[256,256]{1,0:T(8,128)(2,1)S(1)}, bf16[256,256]{1,0:T(8,128)(2,1)}, u32[]{:S(2)}) copy-start(bf16[256,256]{1,0:T(8,128)(2,1)} %param.14) | copy-start | bytes 393220
  170.4 93.6 %all-to-all-start.1 = ((f32[32,128,256]{2,1,0:T(8,128)}), f32[32,128,256]{2,1,0:T(8,128)}, u32[]{:S(2)}, u32[]{:S(2)}) async-start(f32[32,128,256]{2,1,0:T(8,128)} %bitcast.94), calls=%async_computation.1 | async-start | bytes 8388608 | tf_op jit(solution)/shard_map/all_to_all | solution.py:81
  182.4 3.9 %copy-start.12 = (f32[32]{0:T(128)S(1)}, f32[32]{0:T(128)}, u32[]{:S(2)}) copy-start(f32[32]{0:T(128)} %param.15) | copy-start | bytes 388
  190.4 76.2 %copy-start.3 = (f32[128,2048]{1,0:T(8,128)S(1)}, f32[128,2048]{1,0:T(8,128)}, u32[]{:S(2)}) copy-start(f32[128,2048]{1,0:T(8,128)} %copy.64) | copy-start | bytes 3145732
  264.0 2.6 copy-start.5
  266.6 2.4 copy-start.4
  266.6 2.4 copy-start.6
